TPU v7x, 512 devices: a whole 4x8x8 slice. The times are simulated.
512 devices in a mesh: tm: 32 (over y, x), rows: 16 (over z, core).
Axes of the slice: x: 4, y: 8, z: 8, core: 2. Of those that a mesh axis runs over, the one named last changes fastest.
Arguments:
- features: bfloat16 [64, 16, 40, 384], P('tm', 'rows'), may hold values from -6 to 6
- gain_one: float32 [384], replicated, may hold values from 0.1 to 1.9
- weight_one: bfloat16 [384, 3, 3, 3, 384], P('rows'), may hold values from -0.0625 to 0.0625
- bias_one: float32 [384], replicated, may hold values from -3 to 3
- gain_two: float32 [384], replicated, may hold values from 0.1 to 1.9
- weight_two: bfloat16 [384, 3, 3, 3, 384], P('rows'), may hold values from -0.0625 to 0.0625
- bias_two: float32 [384], replicated, may hold values from -3 to 3
Outputs:
- block_out: bfloat16 [64, 16, 40, 384], P('tm', 'rows')
All inputs are finite; a program needn't handle non-finite values.
Results may differ from a plain program's by a relative error of at most 0.0049.
Values may be sent and summed in bfloat16 or wider, within the bound.
No kernel may reach another device: no remote copies, remote signals or barrier semaphores. Data moves between devices by JAX's collectives and lax.ppermute only.
A program may use at most 64 MiB of HBM per device.

v0:
```python
import jax
import jax.numpy as jnp
from jax import lax
from jax.sharding import PartitionSpec as P


def passed_along(x, axis, by):
    peers = lax.axis_size(axis)
    pairs = [(i, i + by) for i in range(peers) if 0 <= i + by < peers]
    return lax.ppermute(x, axis, pairs)


def norm_silu(values, norm_gain):
    values = values.astype(jnp.float32)
    mean_square = jnp.mean(values * values, axis=-1, keepdims=True)
    scaled = values * lax.rsqrt(mean_square + 1e-06) * norm_gain
    return jax.nn.silu(scaled).astype(jnp.bfloat16)


def causal_conv(own, kernel, bias_part):
    part_width = kernel.shape[0]
    frames, height, columns, _ = own.shape
    stacked = jnp.transpose(kernel, (1, 0, 2, 3, 4)).reshape(3 * part_width, 3, 3, kernel.shape[4])
    product = lax.conv_general_dilated(
        own,
        stacked,
        window_strides=(1, 1),
        padding=((1, 1), (1, 1)),
        dimension_numbers=("NHWC", "OHWI", "NHWC"),
        preferred_element_type=jnp.float32,
    )
    tap = [product[..., a * part_width : (a + 1) * part_width] for a in range(3)]

    def rows_first(pair):
        return jnp.transpose(jnp.stack(pair, 0), (1, 0, 2, 3)).reshape(height, frames, -1)

    onward = rows_first([tap[0][0] + tap[1][1], tap[0][1]])
    kept = rows_first([tap[2][0], tap[1][0] + tap[2][1]]) + jnp.tile(bias_part, columns)
    kept = lax.optimization_barrier(kept)
    arrived = passed_along(onward.reshape(height, -1), "tm", 1).reshape(kept.shape)
    return kept + arrived


def own_row(laid, frames, columns):
    sources = lax.all_to_all(laid, "rows", split_axis=0, concat_axis=0, tiled=True)
    sources = sources.reshape(sources.shape[0], frames, columns, -1)
    return jnp.transpose(sources, (1, 2, 0, 3)).reshape(frames, 1, columns, -1)


def shards(features, gain_one, weight_one, bias_one, gain_two, weight_two, bias_two):
    part_width = weight_one.shape[0]
    frames, _, columns, _ = features.shape
    offset = lax.axis_index("rows") * part_width
    bias_first = lax.dynamic_slice_in_dim(bias_one, offset, part_width, 0)
    bias_second = lax.dynamic_slice_in_dim(bias_two, offset, part_width, 0)
    every_row = lax.all_gather(features, "rows", axis=1, tiled=True)
    full_one = norm_silu(every_row, gain_one)
    residual = lax.dynamic_slice_in_dim(every_row, offset, part_width, 3)
    residual = jnp.transpose(residual, (1, 0, 2, 3)).reshape(residual.shape[1], frames, -1)
    conv_one = causal_conv(full_one, weight_one, bias_first).astype(jnp.bfloat16)
    own_rows = own_row(conv_one, frames, columns)
    normed_two = norm_silu(own_rows, gain_two)
    full_two = lax.all_gather(normed_two, "rows", axis=1, tiled=True)
    conv_two = causal_conv(full_two, weight_two, bias_second)
    block_out = (residual.astype(jnp.float32) + conv_two).astype(jnp.bfloat16)
    return own_row(block_out, frames, columns)


def solution(mesh):
    in_specs = (
        P("tm", "rows", None, None),
        P(),
        P("rows", None, None, None, None),
        P(),
        P(),
        P("rows", None, None, None, None),
        P(),
    )
    out_specs = P("tm", "rows", None, None)
    return jax.shard_map(shards, mesh=mesh, in_specs=in_specs, out_specs=out_specs, check_vma=False)
```

profile of v0, /device:TPU:33, one launch (start us, length us, event | category | flops | bytes accessed | tf_op | source)
XLA Modules:
  0.0 105.6 jit_solution(14117151031554257215)
XLA Ops:
  0.0 26.8 %all_gather.6 = bf16[2,16,40,384]{3,2,0,1:T(8,128)(2,1)S(1)} all-gather(bf16[2,1,40,384]{3,2,0,1:T(8,128)(2,1)} %bitcast.79), channel_id=1, replica_groups=mesh['tm'=32,'rows'=16] {'rows'}, dimensions={1}, use_global_device_ids=true | all-gather | bytes 1044480 | tf_op jit(solution)/shard_map/all_gather | solution.py:56
  27.1 0.7 fusion.24
  28.2 0.8 copy-done
  29.0 3.5 %fusion.18 = f32[16,16,6,72]{3,1,2,0:T(8,128)S(1)} fusion(bf16[72,3,3,384]{3,0,2,1:T(8,128)(2,1)S(1)} %bitcast.78, bf16[16,2,8,8,384]{4,0,3,2,1:T(8,128)(2,1)S(1)} %fusion.10, pred[16,6]{0,1:T(8,128)(4,1)S(1)} %copy-done.4), kind=kOutput, calls=%fused_computation.21 | convolution fusion | flops 732672000 | bytes 2512992 | tf_op jit(solution)/shard_map/conv_general_dilated | solution.py:24
  32.5 0.5 copy.74
  33.0 0.4 slice_add_fusion.2
  33.8 0.3 reshape_reshape.6
  34.1 3.1 %collective-permute-start = (f32[16,1920]{1,0:T(8,128)S(1)}, f32[16,1920]{1,0:T(8,128)S(1)}, u32[]{:S(2)}, u32[]{:S(2)}) collective-permute-start(f32[16,1920]{1,0:T(8,128)S(1)} %reshape_reshape.6), channel_id=1, source_target_pairs={{0,16},{16,32},{32,48},{48,64},{64,80},{80,96},{96,112},{112,128},... | collective-permute-start | bytes 368648 | tf_op jit(solution)/shard_map/ppermute | solution.py:10
  37.7 0.8 dynamic_slice.10
  38.6 0.8 dynamic_slice.11
  39.5 4.6 %collective-permute-done = f32[16,1920]{1,0:T(8,128)S(1)} collective-permute-done((f32[16,1920]{1,0:T(8,128)S(1)}, f32[16,1920]{1,0:T(8,128)S(1)}, u32[]{:S(2)}, u32[]{:S(2)}) %collective-permute-start) | collective-permute-done | bytes 122912 | tf_op jit(solution)/shard_map/ppermute | solution.py:10
  44.3 0.7 copy.78
  45.0 4.2 %all-to-all-start = ((bf16[16,2,960]{2,1,0:T(2,128)(2,1)}), bf16[16,2,960]{2,1,0:T(2,128)(2,1)S(1)}, u32[]{:S(2)}, u32[]{:S(2)}) async-start(bf16[16,2,960]{2,1,0:T(2,128)(2,1)} %copy.78), calls=%async_computation | async-start | bytes 131072 | tf_op jit(solution)/shard_map/all_to_all | solution.py:45
  49.4 0.4 reshape.142
  49.8 7.2 %all-to-all-done = bf16[16,2,960]{2,1,0:T(2,128)(2,1)S(1)} async-done(((bf16[16,2,960]{2,1,0:T(2,128)(2,1)}), bf16[16,2,960]{2,1,0:T(2,128)(2,1)S(1)}, u32[]{:S(2)}, u32[]{:S(2)}) %all-to-all-start) | async-done | bytes 61472 | tf_op jit(solution)/shard_map/all_to_all | solution.py:45
  58.1 17.6 %all_gather.7 = bf16[2,16,40,384]{3,2,0,1:T(8,128)(2,1)S(1)} all-gather(bf16[2,1,40,384]{3,2,0,1:T(8,128)(2,1)S(1)} %fusion.27), channel_id=1, replica_groups=mesh['tm'=32,'rows'=16] {'rows'}, dimensions={1}, use_global_device_ids=true | all-gather | bytes 1044480 | tf_op jit(solution)/shard_map/all_gather | solution.py:63
  76.3 3.5 %fusion.21 = f32[16,16,6,72]{3,1,2,0:T(8,128)S(1)} fusion(bf16[72,3,3,384]{3,0,2,1:T(8,128)(2,1)S(1)} %bitcast.77, bf16[16,2,8,8,384]{4,0,3,2,1:T(8,128)(2,1)S(1)} %fusion.11, pred[16,6]{0,1:T(8,128)(4,1)S(1)} %copy-done.4), kind=kOutput, calls=%fused_computation.22 | convolution fusion | flops 732672000 | bytes 2512992 | tf_op jit(solution)/shard_map/conv_general_dilated | solution.py:24
  79.8 0.5 copy.86
  80.3 0.4 slice_add_fusion
  81.0 0.3 reshape_reshape.7
  81.3 1.9 %collective-permute-start.1 = (f32[16,1920]{1,0:T(8,128)S(1)}, f32[16,1920]{1,0:T(8,128)S(1)}, u32[]{:S(2)}, u32[]{:S(2)}) collective-permute-start(f32[16,1920]{1,0:T(8,128)S(1)} %reshape_reshape.7), channel_id=1, source_target_pairs={{0,16},{16,32},{32,48},{48,64},{64,80},{80,96},{96,112},{112,128},... | collective-permute-start | bytes 368648 | tf_op jit(solution)/shard_map/ppermute | solution.py:10
  83.8 7.5 %collective-permute-done.1 = f32[16,1920]{1,0:T(8,128)S(1)} collective-permute-done((f32[16,1920]{1,0:T(8,128)S(1)}, f32[16,1920]{1,0:T(8,128)S(1)}, u32[]{:S(2)}, u32[]{:S(2)}) %collective-permute-start.1) | collective-permute-done | bytes 122912 | tf_op jit(solution)/shard_map/ppermute | solution.py:10
  91.6 12.7 %all_to_all.10 = bf16[16,2,960]{2,1,0:T(2,128)(2,1)S(1)} all-to-all(bf16[16,2,960]{2,1,0:T(2,128)(2,1)S(1)} %copy.90), channel_id=1, replica_groups=mesh['tm'=32,'rows'=16] {'rows'}, dimensions={0} | all-to-all | bytes 122880 | tf_op jit(solution)/shard_map/all_to_all | solution.py:45
  104.9 0.7 copy.93
  (55 shorter events, 5.3 us)
Async XLA Ops:
  0.0 27.1 %copy-start.2 = (f32[384]{0:T(512)S(1)}, f32[384]{0:T(512)}, u32[]{:S(2)}) copy-start(f32[384]{0:T(512)} %param.8) | copy-start | bytes 4612
  27.9 1.0 copy-start
  28.0 1.1 %copy-start.4 = (pred[16,6]{0,1:T(8,128)(4,1)S(1)}, pred[16,6]{0,1:T(8,128)(4,1)}, u32[]{:S(2)}) copy-start(pred[16,6]{0,1:T(8,128)(4,1)} %constant.36) | copy-start | bytes 292
  33.8 4.8 %copy-start.1 = (bf16[24,3,3,3,384]{4,0,3,2,1:T(8,128)(2,1)S(1)}, bf16[24,3,3,3,384]{4,0,3,2,1:T(8,128)(2,1)}, u32[]{:S(2)}) copy-start(bf16[24,3,3,3,384]{4,0,3,2,1:T(8,128)(2,1)} %param.12) | copy-start | bytes 1492996
  34.1 10.0 %collective-permute-start = (f32[16,1920]{1,0:T(8,128)S(1)}, f32[16,1920]{1,0:T(8,128)S(1)}, u32[]{:S(2)}, u32[]{:S(2)}) collective-permute-start(f32[16,1920]{1,0:T(8,128)S(1)} %reshape_reshape.6), channel_id=1, source_target_pairs={{0,16},{16,32},{32,48},{48,64},{64,80},{80,96},{96,112},{112,128},... | collective-permute-start | bytes 368648 | tf_op jit(solution)/shard_map/ppermute | solution.py:10
  45.0 12.1 %all-to-all-start = ((bf16[16,2,960]{2,1,0:T(2,128)(2,1)}), bf16[16,2,960]{2,1,0:T(2,128)(2,1)S(1)}, u32[]{:S(2)}, u32[]{:S(2)}) async-start(bf16[16,2,960]{2,1,0:T(2,128)(2,1)} %copy.78), calls=%async_computation | async-start | bytes 131072 | tf_op jit(solution)/shard_map/all_to_all | solution.py:45
  49.4 8.6 %copy-start.3 = (f32[384]{0:T(512)S(1)}, f32[384]{0:T(512)}, u32[]{:S(2)}) copy-start(f32[384]{0:T(512)} %param.11) | copy-start | bytes 4612
  81.3 10.0 %collective-permute-start.1 = (f32[16,1920]{1,0:T(8,128)S(1)}, f32[16,1920]{1,0:T(8,128)S(1)}, u32[]{:S(2)}, u32[]{:S(2)}) collective-permute-start(f32[16,1920]{1,0:T(8,128)S(1)} %reshape_reshape.7), channel_id=1, source_target_pairs={{0,16},{16,32},{32,48},{48,64},{64,80},{80,96},{96,112},{112,128},... | collective-permute-start | bytes 368648 | tf_op jit(solution)/shard_map/ppermute | solution.py:10
where the time goes:
time: 106 us
  blocking collectives  57.1 us (54%)
  waiting for transfers between devices  19.4 us (18%)
  local copies, waits for them, and re-layouts  9.42 us (9%)
  starting transfers between devices  9.28 us (9%)
  matrix products  6.95 us (7%)
  other arithmetic  3.01 us (3%)
    all_gather x1, blocking collectives, shards(): every_row = lax.all_gather(features, 'rows', axis=1, tiled=True)  26.8 us
    all_gather x1, blocking collectives, shards(): full_two = lax.all_gather(normed_two, 'rows', axis=1, tiled=True)  17.6 us
    all_to_all x1, blocking collectives, own_row(): lax.all_to_all(laid, 'rows', split_axis=0, concat_axis=0, tiled=True)  12.7 us
    ppermute x2, waiting for transfers between devices, passed_along(): return lax.ppermute(x, axis, pairs)  12.1 us
    all_to_all x1, waiting for transfers between devices, own_row(): lax.all_to_all(laid, 'rows', split_axis=0, concat_axis=0, tiled=True)  7.24 us
    conv_general_dilated x2, matrix products, causal_conv(): lax.conv_general_dilated(own, stacked, window_strides=(1, 1), padding=((1...  6.95 us
    ppermute x2, starting transfers between devices, passed_along(): return lax.ppermute(x, axis, pairs)  5.04 us
    all_to_all x1, starting transfers between devices, own_row(): lax.all_to_all(laid, 'rows', split_axis=0, concat_axis=0, tiled=True)  4.24 us
  transfers between devices with their start and end apart: 3, of which 3 were waited for; matrix products, arithmetic and copies ran while one was open for 3% of the time, Pallas kernels for 0%

commit v1 on v0

--- a/solution.py
+++ b/solution.py
@@ -2,6 +2,22 @@
 import jax.numpy as jnp
 from jax import lax
 from jax.sharding import PartitionSpec as P
+
+
+def swapped_with_each(value, axis, split, join):
+    ways, here = (lax.axis_size(axis), lax.axis_index(axis))
+    width = value.shape[split] // ways
+    dims = list(value.shape)
+    dims[split] = width
+    height = dims[join]
+    dims[join] = height * ways
+    full = jnp.zeros(dims, value.dtype)
+    for mask in range(ways):
+        part = lax.dynamic_slice_in_dim(value, (here ^ mask) * width, width, axis=split)
+        if mask:
+            part = lax.ppermute(part, axis, [(d, d ^ mask) for d in range(ways)])
+        full = lax.dynamic_update_slice_in_dim(full, part, (here ^ mask) * height, axis=join)
+    return full
 
 
 def passed_along(x, axis, by):
@@ -42,7 +58,7 @@
 
 
 def own_row(laid, frames, columns):
-    sources = lax.all_to_all(laid, "rows", split_axis=0, concat_axis=0, tiled=True)
+    sources = swapped_with_each(laid, "rows", 0, 0)
     sources = sources.reshape(sources.shape[0], frames, columns, -1)
     return jnp.transpose(sources, (1, 2, 0, 3)).reshape(frames, 1, columns, -1)
 

time: 106 us -> 198 us (1.87)
  the two profiles are of different devices: /device:TPU:33 before, /device:TPU:97 now
where the time goes in v1:
time: 198 us; the launch traced here: 197 us
  starting transfers between devices  115 us (58%)
  blocking collectives  40.9 us (21%)
  waiting for transfers between devices  18 us (9%)
  local copies, waits for them, and re-layouts  11.7 us (6%)
  matrix products  6.96 us (4%)
  other arithmetic  3 us (2%)
    ppermute x30, starting transfers between devices, swapped_with_each(): part = lax.ppermute(part, axis, [(d, d ^ mask) for d in range(ways)])  110 us
    all_gather x1, blocking collectives, shards(): every_row = lax.all_gather(features, 'rows', axis=1, tiled=True)  23.7 us
    all_gather x1, blocking collectives, shards(): full_two = lax.all_gather(normed_two, 'rows', axis=1, tiled=True)  17.3 us
    ppermute x2, waiting for transfers between devices, passed_along(): return lax.ppermute(x, axis, pairs)  12.9 us
    conv_general_dilated x2, matrix products, causal_conv(): lax.conv_general_dilated(own, stacked, window_strides=(1, 1), padding=((1...  6.96 us
    ppermute x30, waiting for transfers between devices, swapped_with_each(): part = lax.ppermute(part, axis, [(d, d ^ mask) for d in range(ways)])  5.05 us
    ppermute x2, starting transfers between devices, passed_along(): return lax.ppermute(x, axis, pairs)  5.03 us
  transfers between devices with their start and end apart: 32, of which 4 were waited for; matrix products, arithmetic and copies ran while one was open for 3% of the time, Pallas kernels for 0%

profile of v1, /device:TPU:97, one launch (start us, length us, event | category | flops | bytes accessed | tf_op | source)
XLA Modules:
  0.0 197.0 jit_solution(14709368706765248193)
XLA Ops:
  0.0 23.7 %all_gather.6 = bf16[2,16,40,384]{3,2,0,1:T(8,128)(2,1)S(1)} all-gather(bf16[2,1,40,384]{3,2,0,1:T(8,128)(2,1)} %bitcast.79), channel_id=1, replica_groups=mesh['tm'=32,'rows'=16] {'rows'}, dimensions={1}, use_global_device_ids=true | all-gather | bytes 1044480 | tf_op jit(solution)/shard_map/all_gather | solution.py:72
  25.9 3.5 %fusion.18 = f32[16,16,6,72]{3,1,2,0:T(8,128)S(1)} fusion(bf16[72,3,3,384]{3,0,2,1:T(8,128)(2,1)S(1)} %bitcast.78, bf16[16,2,8,8,384]{4,0,3,2,1:T(8,128)(2,1)S(1)} %fusion.10, pred[16,6]{0,1:T(8,128)(4,1)S(1)} %copy-done.4), kind=kOutput, calls=%fused_computation.21 | convolution fusion | flops 732672000 | bytes 2512992 | tf_op jit(solution)/shard_map/conv_general_dilated | solution.py:40
  35.6 5.4 %collective-permute-done = f32[16,1920]{1,0:T(8,128)S(1)} collective-permute-done((f32[16,1920]{1,0:T(8,128)S(1)}, f32[16,1920]{1,0:T(8,128)S(1)}, u32[]{:S(2)}, u32[]{:S(2)}) %collective-permute-start) | collective-permute-done | bytes 122912 | tf_op jit(solution)/shard_map/ppermute | solution.py:26
  44.3 4.4 %collective-permute-start.2 = (bf16[1,2,960]{2,0,1:T(2,128)(2,1)S(1)}, bf16[1,2,960]{2,0,1:T(2,128)(2,1)S(1)}, u32[]{:S(2)}, u32[]{:S(2)}) collective-permute-start(bf16[1,2,960]{2,0,1:T(2,128)(2,1)S(1)} %get-tuple-element.42), channel_id=1, source_target_pairs={{0,2},{1,3},{2,0},{3,1},{4,6},{5,7},{6,4},{7,5},{8,10},{9,11},{10,... | collective-permute-start | bytes 11528 | tf_op jit(solution)/shard_map/ppermute | solution.py:18
  52.6 4.8 %collective-permute-start.5 = (bf16[1,2,960]{2,0,1:T(2,128)(2,1)S(1)}, bf16[1,2,960]{2,0,1:T(2,128)(2,1)S(1)}, u32[]{:S(2)}, u32[]{:S(2)}) collective-permute-start(bf16[1,2,960]{2,0,1:T(2,128)(2,1)S(1)} %get-tuple-element.39), channel_id=1, source_target_pairs={{0,5},{1,4},{2,7},{3,6},{4,1},{5,0},{6,3},{7,2},{8,13},{9,12},{10,... | collective-permute-start | bytes 11528 | tf_op jit(solution)/shard_map/ppermute | solution.py:18
  62.7 3.5 %collective-permute-start.8 = (bf16[1,2,960]{2,0,1:T(2,128)(2,1)S(1)}, bf16[1,2,960]{2,0,1:T(2,128)(2,1)S(1)}, u32[]{:S(2)}, u32[]{:S(2)}) collective-permute-start(bf16[1,2,960]{2,0,1:T(2,128)(2,1)S(1)} %get-tuple-element.36), channel_id=1, source_target_pairs={{0,8},{1,9},{2,10},{3,11},{4,12},{5,13},{6,14},{7,15},{8,0},{9,1},... | collective-permute-start | bytes 11528 | tf_op jit(solution)/shard_map/ppermute | solution.py:18
  66.2 6.3 %collective-permute-start.9 = (bf16[1,2,960]{2,0,1:T(2,128)(2,1)S(1)}, bf16[1,2,960]{2,0,1:T(2,128)(2,1)S(1)}, u32[]{:S(2)}, u32[]{:S(2)}) collective-permute-start(bf16[1,2,960]{2,0,1:T(2,128)(2,1)S(1)} %get-tuple-element.35), channel_id=1, source_target_pairs={{0,9},{1,8},{2,11},{3,10},{4,13},{5,12},{6,15},{7,14},{8,1},{9,0},... | collective-permute-start | bytes 11528 | tf_op jit(solution)/shard_map/ppermute | solution.py:18
  72.5 5.0 %collective-permute-start.10 = (bf16[1,2,960]{2,0,1:T(2,128)(2,1)S(1)}, bf16[1,2,960]{2,0,1:T(2,128)(2,1)S(1)}, u32[]{:S(2)}, u32[]{:S(2)}) collective-permute-start(bf16[1,2,960]{2,0,1:T(2,128)(2,1)S(1)} %get-tuple-element.34), channel_id=1, source_target_pairs={{0,10},{1,11},{2,8},{3,9},{4,14},{5,15},{6,12},{7,13},{8,2},{9,3},... | collective-permute-start | bytes 11528 | tf_op jit(solution)/shard_map/ppermute | solution.py:18
  80.8 4.0 %collective-permute-start.12 = (bf16[1,2,960]{2,0,1:T(2,128)(2,1)S(1)}, bf16[1,2,960]{2,0,1:T(2,128)(2,1)S(1)}, u32[]{:S(2)}, u32[]{:S(2)}) collective-permute-start(bf16[1,2,960]{2,0,1:T(2,128)(2,1)S(1)} %get-tuple-element.32), channel_id=1, source_target_pairs={{0,12},{1,13},{2,14},{3,15},{4,8},{5,9},{6,10},{7,11},{8,4},{9,5},... | collective-permute-start | bytes 11528 | tf_op jit(solution)/shard_map/ppermute | solution.py:18
  84.9 4.0 %collective-permute-start.13 = (bf16[1,2,960]{2,0,1:T(2,128)(2,1)S(1)}, bf16[1,2,960]{2,0,1:T(2,128)(2,1)S(1)}, u32[]{:S(2)}, u32[]{:S(2)}) collective-permute-start(bf16[1,2,960]{2,0,1:T(2,128)(2,1)S(1)} %get-tuple-element.31), channel_id=1, source_target_pairs={{0,13},{1,12},{2,15},{3,14},{4,9},{5,8},{6,11},{7,10},{8,5},{9,4},... | collective-permute-start | bytes 11528 | tf_op jit(solution)/shard_map/ppermute | solution.py:18
  88.9 4.6 %collective-permute-start.14 = (bf16[1,2,960]{2,0,1:T(2,128)(2,1)S(1)}, bf16[1,2,960]{2,0,1:T(2,128)(2,1)S(1)}, u32[]{:S(2)}, u32[]{:S(2)}) collective-permute-start(bf16[1,2,960]{2,0,1:T(2,128)(2,1)S(1)} %get-tuple-element.30), channel_id=1, source_target_pairs={{0,14},{1,15},{2,12},{3,13},{4,10},{5,11},{6,8},{7,9},{8,6},{9,7},... | collective-permute-start | bytes 11528 | tf_op jit(solution)/shard_map/ppermute | solution.py:18
  93.4 3.7 %collective-permute-start.15 = (bf16[1,2,960]{2,0,1:T(2,128)(2,1)S(1)}, bf16[1,2,960]{2,0,1:T(2,128)(2,1)S(1)}, u32[]{:S(2)}, u32[]{:S(2)}) collective-permute-start(bf16[1,2,960]{2,0,1:T(2,128)(2,1)S(1)} %get-tuple-element.29), channel_id=1, source_target_pairs={{0,15},{1,14},{2,13},{3,12},{4,11},{5,10},{6,9},{7,8},{8,7},{9,6},... | collective-permute-start | bytes 11528 | tf_op jit(solution)/shard_map/ppermute | solution.py:18
  102.8 17.3 %all_gather.7 = bf16[2,16,40,384]{3,2,0,1:T(8,128)(2,1)S(1)} all-gather(bf16[2,1,40,384]{3,2,0,1:T(8,128)(2,1)S(1)} %fusion.27), channel_id=1, replica_groups=mesh['tm'=32,'rows'=16] {'rows'}, dimensions={1}, use_global_device_ids=true | all-gather | bytes 1044480 | tf_op jit(solution)/shard_map/all_gather | solution.py:79
  120.7 3.5 %fusion.21 = f32[16,16,6,72]{3,1,2,0:T(8,128)S(1)} fusion(bf16[72,3,3,384]{3,0,2,1:T(8,128)(2,1)S(1)} %bitcast.77, bf16[16,2,8,8,384]{4,0,3,2,1:T(8,128)(2,1)S(1)} %fusion.11, pred[16,6]{0,1:T(8,128)(4,1)S(1)} %copy-done.4), kind=kOutput, calls=%fused_computation.22 | convolution fusion | flops 732672000 | bytes 2512992 | tf_op jit(solution)/shard_map/conv_general_dilated | solution.py:40
  128.2 7.5 %collective-permute-done.16 = f32[16,1920]{1,0:T(8,128)S(1)} collective-permute-done((f32[16,1920]{1,0:T(8,128)S(1)}, f32[16,1920]{1,0:T(8,128)S(1)}, u32[]{:S(2)}, u32[]{:S(2)}) %collective-permute-start.16) | collective-permute-done | bytes 122912 | tf_op jit(solution)/shard_map/ppermute | solution.py:26
  139.1 3.6 %collective-permute-start.18 = (bf16[1,2,960]{2,0,1:T(2,128)(2,1)S(1)}, bf16[1,2,960]{2,0,1:T(2,128)(2,1)S(1)}, u32[]{:S(2)}, u32[]{:S(2)}) collective-permute-start(bf16[1,2,960]{2,0,1:T(2,128)(2,1)S(1)} %get-tuple-element.26), channel_id=1, source_target_pairs={{0,2},{1,3},{2,0},{3,1},{4,6},{5,7},{6,4},{7,5},{8,10},{9,11},{10,... | collective-permute-start | bytes 11528 | tf_op jit(solution)/shard_map/ppermute | solution.py:18
  146.7 4.6 %collective-permute-start.21 = (bf16[1,2,960]{2,0,1:T(2,128)(2,1)S(1)}, bf16[1,2,960]{2,0,1:T(2,128)(2,1)S(1)}, u32[]{:S(2)}, u32[]{:S(2)}) collective-permute-start(bf16[1,2,960]{2,0,1:T(2,128)(2,1)S(1)} %get-tuple-element.23), channel_id=1, source_target_pairs={{0,5},{1,4},{2,7},{3,6},{4,1},{5,0},{6,3},{7,2},{8,13},{9,12},{10,... | collective-permute-start | bytes 11528 | tf_op jit(solution)/shard_map/ppermute | solution.py:18
  156.7 4.2 %collective-permute-start.24 = (bf16[1,2,960]{2,0,1:T(2,128)(2,1)S(1)}, bf16[1,2,960]{2,0,1:T(2,128)(2,1)S(1)}, u32[]{:S(2)}, u32[]{:S(2)}) collective-permute-start(bf16[1,2,960]{2,0,1:T(2,128)(2,1)S(1)} %get-tuple-element.20), channel_id=1, source_target_pairs={{0,8},{1,9},{2,10},{3,11},{4,12},{5,13},{6,14},{7,15},{8,0},{9,1},... | collective-permute-start | bytes 11528 | tf_op jit(solution)/shard_map/ppermute | solution.py:18
  160.9 5.6 %collective-permute-start.25 = (bf16[1,2,960]{2,0,1:T(2,128)(2,1)S(1)}, bf16[1,2,960]{2,0,1:T(2,128)(2,1)S(1)}, u32[]{:S(2)}, u32[]{:S(2)}) collective-permute-start(bf16[1,2,960]{2,0,1:T(2,128)(2,1)S(1)} %get-tuple-element.19), channel_id=1, source_target_pairs={{0,9},{1,8},{2,11},{3,10},{4,13},{5,12},{6,15},{7,14},{8,1},{9,0},... | collective-permute-start | bytes 11528 | tf_op jit(solution)/shard_map/ppermute | solution.py:18
  166.5 6.0 %collective-permute-start.26 = (bf16[1,2,960]{2,0,1:T(2,128)(2,1)S(1)}, bf16[1,2,960]{2,0,1:T(2,128)(2,1)S(1)}, u32[]{:S(2)}, u32[]{:S(2)}) collective-permute-start(bf16[1,2,960]{2,0,1:T(2,128)(2,1)S(1)} %get-tuple-element.18), channel_id=1, source_target_pairs={{0,10},{1,11},{2,8},{3,9},{4,14},{5,15},{6,12},{7,13},{8,2},{9,3},... | collective-permute-start | bytes 11528 | tf_op jit(solution)/shard_map/ppermute | solution.py:18
  174.8 4.8 %collective-permute-start.28 = (bf16[1,2,960]{2,0,1:T(2,128)(2,1)S(1)}, bf16[1,2,960]{2,0,1:T(2,128)(2,1)S(1)}, u32[]{:S(2)}, u32[]{:S(2)}) collective-permute-start(bf16[1,2,960]{2,0,1:T(2,128)(2,1)S(1)} %get-tuple-element.16), channel_id=1, source_target_pairs={{0,12},{1,13},{2,14},{3,15},{4,8},{5,9},{6,10},{7,11},{8,4},{9,5},... | collective-permute-start | bytes 11528 | tf_op jit(solution)/shard_map/ppermute | solution.py:18
  182.8 4.6 %collective-permute-start.30 = (bf16[1,2,960]{2,0,1:T(2,128)(2,1)S(1)}, bf16[1,2,960]{2,0,1:T(2,128)(2,1)S(1)}, u32[]{:S(2)}, u32[]{:S(2)}) collective-permute-start(bf16[1,2,960]{2,0,1:T(2,128)(2,1)S(1)} %get-tuple-element.14), channel_id=1, source_target_pairs={{0,14},{1,15},{2,12},{3,13},{4,10},{5,11},{6,8},{7,9},{8,6},{9,7},... | collective-permute-start | bytes 11528 | tf_op jit(solution)/shard_map/ppermute | solution.py:18
  187.4 3.7 %collective-permute-start.31 = (bf16[1,2,960]{2,0,1:T(2,128)(2,1)S(1)}, bf16[1,2,960]{2,0,1:T(2,128)(2,1)S(1)}, u32[]{:S(2)}, u32[]{:S(2)}) collective-permute-start(bf16[1,2,960]{2,0,1:T(2,128)(2,1)S(1)} %get-tuple-element.13), channel_id=1, source_target_pairs={{0,15},{1,14},{2,13},{3,12},{4,11},{5,10},{6,9},{7,8},{8,7},{9,6},... | collective-permute-start | bytes 11528 | tf_op jit(solution)/shard_map/ppermute | solution.py:18
  192.5 3.3 %collective-permute-done.31 = bf16[1,2,960]{2,0,1:T(2,128)(2,1)S(1)} collective-permute-done((bf16[1,2,960]{2,0,1:T(2,128)(2,1)S(1)}, bf16[1,2,960]{2,0,1:T(2,128)(2,1)S(1)}, u32[]{:S(2)}, u32[]{:S(2)}) %collective-permute-start.31) | collective-permute-done | bytes 3872 | tf_op jit(solution)/shard_map/ppermute | solution.py:18
  (144 shorter events, 54.3 us)
Async XLA Ops:
  41.4 16.0 %collective-permute-start.1 = (bf16[1,2,960]{2,0,1:T(2,128)(2,1)S(1)}, bf16[1,2,960]{2,0,1:T(2,128)(2,1)S(1)}, u32[]{:S(2)}, u32[]{:S(2)}) collective-permute-start(bf16[1,2,960]{2,0,1:T(2,128)(2,1)S(1)} %get-tuple-element.43), channel_id=1, source_target_pairs={{0,1},{1,0},{2,3},{3,2},{4,5},{5,4},{6,7},{7,6},{8,9},{9,8},{10,11... | collective-permute-start | bytes 11528 | tf_op jit(solution)/shard_map/ppermute | solution.py:18
  44.3 15.3 %collective-permute-start.2 = (bf16[1,2,960]{2,0,1:T(2,128)(2,1)S(1)}, bf16[1,2,960]{2,0,1:T(2,128)(2,1)S(1)}, u32[]{:S(2)}, u32[]{:S(2)}) collective-permute-start(bf16[1,2,960]{2,0,1:T(2,128)(2,1)S(1)} %get-tuple-element.42), channel_id=1, source_target_pairs={{0,2},{1,3},{2,0},{3,1},{4,6},{5,7},{6,4},{7,5},{8,10},{9,11},{10,... | collective-permute-start | bytes 11528 | tf_op jit(solution)/shard_map/ppermute | solution.py:18
  48.7 14.0 %collective-permute-start.3 = (bf16[1,2,960]{2,0,1:T(2,128)(2,1)S(1)}, bf16[1,2,960]{2,0,1:T(2,128)(2,1)S(1)}, u32[]{:S(2)}, u32[]{:S(2)}) collective-permute-start(bf16[1,2,960]{2,0,1:T(2,128)(2,1)S(1)} %get-tuple-element.41), channel_id=1, source_target_pairs={{0,3},{1,2},{2,1},{3,0},{4,7},{5,6},{6,5},{7,4},{8,11},{9,10},{10,... | collective-permute-start | bytes 11528 | tf_op jit(solution)/shard_map/ppermute | solution.py:18
  50.6 15.6 %collective-permute-start.4 = (bf16[1,2,960]{2,0,1:T(2,128)(2,1)S(1)}, bf16[1,2,960]{2,0,1:T(2,128)(2,1)S(1)}, u32[]{:S(2)}, u32[]{:S(2)}) collective-permute-start(bf16[1,2,960]{2,0,1:T(2,128)(2,1)S(1)} %get-tuple-element.40), channel_id=1, source_target_pairs={{0,4},{1,5},{2,6},{3,7},{4,0},{5,1},{6,2},{7,3},{8,12},{9,13},{10,... | collective-permute-start | bytes 11528 | tf_op jit(solution)/shard_map/ppermute | solution.py:18
  52.6 19.9 %collective-permute-start.5 = (bf16[1,2,960]{2,0,1:T(2,128)(2,1)S(1)}, bf16[1,2,960]{2,0,1:T(2,128)(2,1)S(1)}, u32[]{:S(2)}, u32[]{:S(2)}) collective-permute-start(bf16[1,2,960]{2,0,1:T(2,128)(2,1)S(1)} %get-tuple-element.39), channel_id=1, source_target_pairs={{0,5},{1,4},{2,7},{3,6},{4,1},{5,0},{6,3},{7,2},{8,13},{9,12},{10,... | collective-permute-start | bytes 11528 | tf_op jit(solution)/shard_map/ppermute | solution.py:18
  57.4 20.2 %collective-permute-start.6 = (bf16[1,2,960]{2,0,1:T(2,128)(2,1)S(1)}, bf16[1,2,960]{2,0,1:T(2,128)(2,1)S(1)}, u32[]{:S(2)}, u32[]{:S(2)}) collective-permute-start(bf16[1,2,960]{2,0,1:T(2,128)(2,1)S(1)} %get-tuple-element.38), channel_id=1, source_target_pairs={{0,6},{1,7},{2,4},{3,5},{4,2},{5,3},{6,0},{7,1},{8,14},{9,15},{10,... | collective-permute-start | bytes 11528 | tf_op jit(solution)/shard_map/ppermute | solution.py:18
  59.6 21.2 %collective-permute-start.7 = (bf16[1,2,960]{2,0,1:T(2,128)(2,1)S(1)}, bf16[1,2,960]{2,0,1:T(2,128)(2,1)S(1)}, u32[]{:S(2)}, u32[]{:S(2)}) collective-permute-start(bf16[1,2,960]{2,0,1:T(2,128)(2,1)S(1)} %get-tuple-element.37), channel_id=1, source_target_pairs={{0,7},{1,6},{2,5},{3,4},{4,3},{5,2},{6,1},{7,0},{8,15},{9,14},{10,... | collective-permute-start | bytes 11528 | tf_op jit(solution)/shard_map/ppermute | solution.py:18
  62.7 22.2 %collective-permute-start.8 = (bf16[1,2,960]{2,0,1:T(2,128)(2,1)S(1)}, bf16[1,2,960]{2,0,1:T(2,128)(2,1)S(1)}, u32[]{:S(2)}, u32[]{:S(2)}) collective-permute-start(bf16[1,2,960]{2,0,1:T(2,128)(2,1)S(1)} %get-tuple-element.36), channel_id=1, source_target_pairs={{0,8},{1,9},{2,10},{3,11},{4,12},{5,13},{6,14},{7,15},{8,0},{9,1},... | collective-permute-start | bytes 11528 | tf_op jit(solution)/shard_map/ppermute | solution.py:18
  66.2 22.6 %collective-permute-start.9 = (bf16[1,2,960]{2,0,1:T(2,128)(2,1)S(1)}, bf16[1,2,960]{2,0,1:T(2,128)(2,1)S(1)}, u32[]{:S(2)}, u32[]{:S(2)}) collective-permute-start(bf16[1,2,960]{2,0,1:T(2,128)(2,1)S(1)} %get-tuple-element.35), channel_id=1, source_target_pairs={{0,9},{1,8},{2,11},{3,10},{4,13},{5,12},{6,15},{7,14},{8,1},{9,0},... | collective-permute-start | bytes 11528 | tf_op jit(solution)/shard_map/ppermute | solution.py:18
  72.5 20.9 %collective-permute-start.10 = (bf16[1,2,960]{2,0,1:T(2,128)(2,1)S(1)}, bf16[1,2,960]{2,0,1:T(2,128)(2,1)S(1)}, u32[]{:S(2)}, u32[]{:S(2)}) collective-permute-start(bf16[1,2,960]{2,0,1:T(2,128)(2,1)S(1)} %get-tuple-element.34), channel_id=1, source_target_pairs={{0,10},{1,11},{2,8},{3,9},{4,14},{5,15},{6,12},{7,13},{8,2},{9,3},... | collective-permute-start | bytes 11528 | tf_op jit(solution)/shard_map/ppermute | solution.py:18
  77.6 22.1 %collective-permute-start.11 = (bf16[1,2,960]{2,0,1:T(2,128)(2,1)S(1)}, bf16[1,2,960]{2,0,1:T(2,128)(2,1)S(1)}, u32[]{:S(2)}, u32[]{:S(2)}) collective-permute-start(bf16[1,2,960]{2,0,1:T(2,128)(2,1)S(1)} %get-tuple-element.33), channel_id=1, source_target_pairs={{0,11},{1,10},{2,9},{3,8},{4,15},{5,14},{6,13},{7,12},{8,3},{9,2},... | collective-permute-start | bytes 11528 | tf_op jit(solution)/shard_map/ppermute | solution.py:18
  80.8 18.9 %collective-permute-start.12 = (bf16[1,2,960]{2,0,1:T(2,128)(2,1)S(1)}, bf16[1,2,960]{2,0,1:T(2,128)(2,1)S(1)}, u32[]{:S(2)}, u32[]{:S(2)}) collective-permute-start(bf16[1,2,960]{2,0,1:T(2,128)(2,1)S(1)} %get-tuple-element.32), channel_id=1, source_target_pairs={{0,12},{1,13},{2,14},{3,15},{4,8},{5,9},{6,10},{7,11},{8,4},{9,5},... | collective-permute-start | bytes 11528 | tf_op jit(solution)/shard_map/ppermute | solution.py:18
  84.9 15.0 %collective-permute-start.13 = (bf16[1,2,960]{2,0,1:T(2,128)(2,1)S(1)}, bf16[1,2,960]{2,0,1:T(2,128)(2,1)S(1)}, u32[]{:S(2)}, u32[]{:S(2)}) collective-permute-start(bf16[1,2,960]{2,0,1:T(2,128)(2,1)S(1)} %get-tuple-element.31), channel_id=1, source_target_pairs={{0,13},{1,12},{2,15},{3,14},{4,9},{5,8},{6,11},{7,10},{8,5},{9,4},... | collective-permute-start | bytes 11528 | tf_op jit(solution)/shard_map/ppermute | solution.py:18
  136.2 15.2 %collective-permute-start.17 = (bf16[1,2,960]{2,0,1:T(2,128)(2,1)S(1)}, bf16[1,2,960]{2,0,1:T(2,128)(2,1)S(1)}, u32[]{:S(2)}, u32[]{:S(2)}) collective-permute-start(bf16[1,2,960]{2,0,1:T(2,128)(2,1)S(1)} %get-tuple-element.27), channel_id=1, source_target_pairs={{0,1},{1,0},{2,3},{3,2},{4,5},{5,4},{6,7},{7,6},{8,9},{9,8},{10,11... | collective-permute-start | bytes 11528 | tf_op jit(solution)/shard_map/ppermute | solution.py:18
  139.1 14.6 %collective-permute-start.18 = (bf16[1,2,960]{2,0,1:T(2,128)(2,1)S(1)}, bf16[1,2,960]{2,0,1:T(2,128)(2,1)S(1)}, u32[]{:S(2)}, u32[]{:S(2)}) collective-permute-start(bf16[1,2,960]{2,0,1:T(2,128)(2,1)S(1)} %get-tuple-element.26), channel_id=1, source_target_pairs={{0,2},{1,3},{2,0},{3,1},{4,6},{5,7},{6,4},{7,5},{8,10},{9,11},{10,... | collective-permute-start | bytes 11528 | tf_op jit(solution)/shard_map/ppermute | solution.py:18
  144.6 16.3 %collective-permute-start.20 = (bf16[1,2,960]{2,0,1:T(2,128)(2,1)S(1)}, bf16[1,2,960]{2,0,1:T(2,128)(2,1)S(1)}, u32[]{:S(2)}, u32[]{:S(2)}) collective-permute-start(bf16[1,2,960]{2,0,1:T(2,128)(2,1)S(1)} %get-tuple-element.24), channel_id=1, source_target_pairs={{0,4},{1,5},{2,6},{3,7},{4,0},{5,1},{6,2},{7,3},{8,12},{9,13},{10,... | collective-permute-start | bytes 11528 | tf_op jit(solution)/shard_map/ppermute | solution.py:18
  146.7 19.8 %collective-permute-start.21 = (bf16[1,2,960]{2,0,1:T(2,128)(2,1)S(1)}, bf16[1,2,960]{2,0,1:T(2,128)(2,1)S(1)}, u32[]{:S(2)}, u32[]{:S(2)}) collective-permute-start(bf16[1,2,960]{2,0,1:T(2,128)(2,1)S(1)} %get-tuple-element.23), channel_id=1, source_target_pairs={{0,5},{1,4},{2,7},{3,6},{4,1},{5,0},{6,3},{7,2},{8,13},{9,12},{10,... | collective-permute-start | bytes 11528 | tf_op jit(solution)/shard_map/ppermute | solution.py:18
  151.4 21.2 %collective-permute-start.22 = (bf16[1,2,960]{2,0,1:T(2,128)(2,1)S(1)}, bf16[1,2,960]{2,0,1:T(2,128)(2,1)S(1)}, u32[]{:S(2)}, u32[]{:S(2)}) collective-permute-start(bf16[1,2,960]{2,0,1:T(2,128)(2,1)S(1)} %get-tuple-element.22), channel_id=1, source_target_pairs={{0,6},{1,7},{2,4},{3,5},{4,2},{5,3},{6,0},{7,1},{8,14},{9,15},{10,... | collective-permute-start | bytes 11528 | tf_op jit(solution)/shard_map/ppermute | solution.py:18
  153.6 21.2 %collective-permute-start.23 = (bf16[1,2,960]{2,0,1:T(2,128)(2,1)S(1)}, bf16[1,2,960]{2,0,1:T(2,128)(2,1)S(1)}, u32[]{:S(2)}, u32[]{:S(2)}) collective-permute-start(bf16[1,2,960]{2,0,1:T(2,128)(2,1)S(1)} %get-tuple-element.21), channel_id=1, source_target_pairs={{0,7},{1,6},{2,5},{3,4},{4,3},{5,2},{6,1},{7,0},{8,15},{9,14},{10,... | collective-permute-start | bytes 11528 | tf_op jit(solution)/shard_map/ppermute | solution.py:18
  156.7 22.9 %collective-permute-start.24 = (bf16[1,2,960]{2,0,1:T(2,128)(2,1)S(1)}, bf16[1,2,960]{2,0,1:T(2,128)(2,1)S(1)}, u32[]{:S(2)}, u32[]{:S(2)}) collective-permute-start(bf16[1,2,960]{2,0,1:T(2,128)(2,1)S(1)} %get-tuple-element.20), channel_id=1, source_target_pairs={{0,8},{1,9},{2,10},{3,11},{4,12},{5,13},{6,14},{7,15},{8,0},{9,1},... | collective-permute-start | bytes 11528 | tf_op jit(solution)/shard_map/ppermute | solution.py:18
  160.9 21.9 %collective-permute-start.25 = (bf16[1,2,960]{2,0,1:T(2,128)(2,1)S(1)}, bf16[1,2,960]{2,0,1:T(2,128)(2,1)S(1)}, u32[]{:S(2)}, u32[]{:S(2)}) collective-permute-start(bf16[1,2,960]{2,0,1:T(2,128)(2,1)S(1)} %get-tuple-element.19), channel_id=1, source_target_pairs={{0,9},{1,8},{2,11},{3,10},{4,13},{5,12},{6,15},{7,14},{8,1},{9,0},... | collective-permute-start | bytes 11528 | tf_op jit(solution)/shard_map/ppermute | solution.py:18
  166.5 20.9 %collective-permute-start.26 = (bf16[1,2,960]{2,0,1:T(2,128)(2,1)S(1)}, bf16[1,2,960]{2,0,1:T(2,128)(2,1)S(1)}, u32[]{:S(2)}, u32[]{:S(2)}) collective-permute-start(bf16[1,2,960]{2,0,1:T(2,128)(2,1)S(1)} %get-tuple-element.18), channel_id=1, source_target_pairs={{0,10},{1,11},{2,8},{3,9},{4,14},{5,15},{6,12},{7,13},{8,2},{9,3},... | collective-permute-start | bytes 11528 | tf_op jit(solution)/shard_map/ppermute | solution.py:18
  172.6 19.5 %collective-permute-start.27 = (bf16[1,2,960]{2,0,1:T(2,128)(2,1)S(1)}, bf16[1,2,960]{2,0,1:T(2,128)(2,1)S(1)}, u32[]{:S(2)}, u32[]{:S(2)}) collective-permute-start(bf16[1,2,960]{2,0,1:T(2,128)(2,1)S(1)} %get-tuple-element.17), channel_id=1, source_target_pairs={{0,11},{1,10},{2,9},{3,8},{4,15},{5,14},{6,13},{7,12},{8,3},{9,2},... | collective-permute-start | bytes 11528 | tf_op jit(solution)/shard_map/ppermute | solution.py:18
  174.8 17.4 %collective-permute-start.28 = (bf16[1,2,960]{2,0,1:T(2,128)(2,1)S(1)}, bf16[1,2,960]{2,0,1:T(2,128)(2,1)S(1)}, u32[]{:S(2)}, u32[]{:S(2)}) collective-permute-start(bf16[1,2,960]{2,0,1:T(2,128)(2,1)S(1)} %get-tuple-element.16), channel_id=1, source_target_pairs={{0,12},{1,13},{2,14},{3,15},{4,8},{5,9},{6,10},{7,11},{8,4},{9,5},... | collective-permute-start | bytes 11528 | tf_op jit(solution)/shard_map/ppermute | solution.py:18
  (13 other events, 176.2 us)
